TPU v7x, 256 devices: a whole 4x4x8 slice. The times are simulated.
256 devices in a mesh: tile: 16 (over y, z_hi), spec: 16 (over x, z_lo, core).
Axes of the slice: x: 4, y: 4, z: 8 (z_hi: 4, z_lo: 2; z = z_hi * 2 + z_lo), core: 2. Of those that a mesh axis runs over, the one named last changes fastest.
Arguments:
- latent: bfloat16 [32, 4096, 1024], P(None, ('tile', 'spec')), may hold values from -6 to 6
- basis: bfloat16 [224, 32], replicated, may hold values from -1 to 1
- response: bfloat16 [8, 224], replicated, may hold values from -0.375 to 0.375
- hyper_obs: bfloat16 [224, 1024, 256], P('spec', 'tile'), may hold values from -6 to 6
- multi_obs: bfloat16 [8, 4096, 1024], P(None, ('tile', 'spec')), may hold values from -6 to 6
Outputs:
- z_next: bfloat16 [32, 4096, 1024], P(None, ('tile', 'spec'))
- hs_residual: bfloat16 [224, 1024, 256], P('spec', 'tile')
All inputs are finite; a program needn't handle non-finite values.
Results may differ from a plain program's by a relative error of at most 0.0054.
Values may be sent and summed in bfloat16 or wider, within the bound.
No kernel may reach another device: no remote copies, remote signals or barrier semaphores. Data moves between devices by JAX's collectives and lax.ppermute only.
A program may use at most 128 MiB of HBM per device.

v0:
```python
import jax
import jax.numpy as jnp
from jax import lax
from jax.sharding import PartitionSpec as P

DECIM = 4
HALO = 128
step_size = 0.3


def with_halo(cells, sides, width):
    for axis, dim in sides:
        count = lax.axis_size(axis)
        ends = count - 1
        head = lax.slice_in_dim(cells, 0, width, axis=dim)
        tail = lax.slice_in_dim(cells, cells.shape[dim] - width, cells.shape[dim], axis=dim)
        cells = jnp.concatenate(
            [
                lax.ppermute(tail, axis, [(i, (i + 1) % count) for i in range(ends)]),
                cells,
                lax.ppermute(head, axis, [((i + 1) % count, i) for i in range(ends)]),
            ],
            axis=dim,
        )
    return cells


def profile(where_at):
    narrow = DECIM / 2.0
    decay_len = 3.0 * HALO / 8.0
    ripple = jnp.cos(where_at * (jnp.pi / 7.0))
    return (
        jnp.exp(-where_at * where_at / (2.0 * narrow * narrow))
        + 0.5 * jnp.exp(-jnp.abs(where_at) / decay_len) * ripple * ripple
    )


def kernel_values(offsets):
    every_offset = jnp.arange(-HALO, HALO + 1).astype(jnp.float32)
    energy = jnp.sqrt(jnp.sum(profile(every_offset) ** 2))
    inside = jnp.abs(offsets) <= HALO
    return jnp.where(inside, profile(offsets.astype(jnp.float32)) / energy, 0.0).astype(
        jnp.bfloat16
    )


def column_matrix(fine_count, coarse_count):
    fine_cols = jnp.arange(fine_count)[:, None]
    coarse = jnp.arange(coarse_count)[None, :]
    return kernel_values(fine_cols - DECIM * coarse)


def row_matrix(rows_local):
    coarse = jnp.arange(rows_local // DECIM)[:, None]
    padded = jnp.arange(rows_local + 2 * HALO)[None, :]
    return kernel_values(padded - HALO - DECIM * coarse)


def back_matrix(rows_local):
    fine_rows = jnp.arange(rows_local)[:, None]
    coarse = jnp.arange(rows_local // DECIM + 2 * (HALO // DECIM))[None, :]
    return kernel_values(fine_rows - DECIM * coarse + HALO)


def shards(latent, basis, response, hyper_obs, multi_obs):
    highest = lax.Precision.HIGHEST
    rows_dev = hyper_obs.shape[1] * DECIM
    width_cols = latent.shape[2]
    spectra = jnp.einsum("bk,krc->brc", basis, latent, preferred_element_type=jnp.float32).astype(
        jnp.bfloat16
    )
    column_kernel = column_matrix(width_cols, width_cols // DECIM)
    column_wide = column_kernel.astype(jnp.float32)
    band_cube = lax.all_to_all(spectra, "spec", split_axis=0, concat_axis=1, tiled=True)
    padded = with_halo(band_cube, (("tile", 1),), HALO)
    rows_done = jnp.einsum(
        "ir,brc->bic", row_matrix(rows_dev), padded, preferred_element_type=jnp.float32
    )
    blurred = jnp.einsum("bic,cj->bij", rows_done, column_wide, precision=highest)
    hs_residual = (blurred - hyper_obs.astype(jnp.float32)).astype(jnp.bfloat16)
    coarse_padded = with_halo(hs_residual, (("tile", 1),), HALO // DECIM)
    rows_back = jnp.einsum(
        "rq,bqj->brj", back_matrix(rows_dev), coarse_padded, preferred_element_type=jnp.float32
    )
    multi_resid = (
        jnp.einsum("mb,brc->mrc", response, spectra, preferred_element_type=jnp.float32)
        - multi_obs.astype(jnp.float32)
    ).astype(jnp.bfloat16)
    spread = jnp.einsum("brj,cj->brc", rows_back, column_wide, precision=highest).astype(
        jnp.bfloat16
    )
    spread_pixel = lax.all_to_all(spread, "spec", split_axis=1, concat_axis=0, tiled=True)
    multi_back = jnp.einsum(
        "mb,mrc->brc", response, multi_resid, preferred_element_type=jnp.float32
    )
    spectral = (spread_pixel.astype(jnp.float32) + multi_back).astype(jnp.bfloat16)
    gradient = jnp.einsum("bk,brc->krc", basis, spectral, preferred_element_type=jnp.float32)
    z_next = (latent.astype(jnp.float32) - step_size * gradient).astype(jnp.bfloat16)
    return (z_next, hs_residual)


def solution(mesh):
    in_specs = (
        P(None, ("tile", "spec"), None),
        P(),
        P(),
        P("spec", "tile", None),
        P(None, ("tile", "spec"), None),
    )
    out_specs = (P(None, ("tile", "spec"), None), P("spec", "tile", None))
    return jax.shard_map(shards, mesh=mesh, in_specs=in_specs, out_specs=out_specs, check_vma=False)
```

profile of v0, /device:TPU:16, one launch (start us, length us, event | category | flops | bytes accessed | tf_op | source)
XLA Modules:
  0.0 485.2 jit_solution(12088717307099178395)
XLA Ops:
  0.6 0.0 copy-start
  0.6 0.7 copy-done
  1.4 3.3 convolution_convert_fusion.1
  4.7 0.0 copy-start.1
  4.7 7.1 %copy.30 = bf16[224,16,1024]{2,1,0:T(8,128)(2,1)} copy(bf16[224,16,1024]{2,0,1:T(8,128)(2,1)S(1)} %convolution_convert_fusion.1) | data formatting | bytes 14680064 | tf_op jit(solution)/shard_map/convert_element_type | solution.py:69
  11.8 0.0 copy-done.1
  11.8 89.8 %all_to_all.27 = bf16[224,16,1024]{2,1,0:T(8,128)(2,1)} all-to-all(bf16[224,16,1024]{2,1,0:T(8,128)(2,1)} %copy.30), channel_id=1, replica_groups=mesh['tile'=16,'spec'=16] {'spec'}, dimensions={0} | all-to-all | bytes 14680064 | tf_op jit(solution)/shard_map/all_to_all | solution.py:74
  101.6 4.7 copy.31
  106.3 0.0 copy-start.2
  106.3 4.8 fusion.119
  111.1 0.9 copy-done.2
  112.0 5.2 %collective-permute-start = (bf16[14,128,1024]{2,1,0:T(8,128)(2,1)}, bf16[14,128,1024]{2,1,0:T(8,128)(2,1)}, u32[]{:S(2)}, u32[]{:S(2)}) collective-permute-start(bf16[14,128,1024]{2,1,0:T(8,128)(2,1)} %get-tuple-element.10), channel_id=1, source_target_pairs={{0,16},{16,32},{32,48},{48,64},{64,80},{80,96},{96,112},{112,128},... | collective-permute-start | bytes 11010056 | tf_op jit(solution)/shard_map/ppermute | solution.py:19
  117.2 4.1 collective-permute-start.1
  121.3 0.7 fusion.92
  122.7 0.0 copy-start.7
  122.7 76.3 %collective-permute-done = bf16[14,128,1024]{2,1,0:T(8,128)(2,1)} collective-permute-done((bf16[14,128,1024]{2,1,0:T(8,128)(2,1)}, bf16[14,128,1024]{2,1,0:T(8,128)(2,1)}, u32[]{:S(2)}, u32[]{:S(2)}) %collective-permute-start) | collective-permute-done | bytes 3670048 | tf_op jit(solution)/shard_map/ppermute | solution.py:19
  199.0 64.5 %collective-permute-done.1 = bf16[14,128,1024]{2,1,0:T(8,128)(2,1)} collective-permute-done((bf16[14,128,1024]{2,1,0:T(8,128)(2,1)}, bf16[14,128,1024]{2,1,0:T(8,128)(2,1)}, u32[]{:S(2)}, u32[]{:S(2)}) %collective-permute-start.1) | collective-permute-done | bytes 3670048 | tf_op jit(solution)/shard_map/ppermute | solution.py:21
  263.5 8.2 %fusion = f32[14,1024,64]{1,2,0:T(8,128)S(1)} fusion(bf16[14,128,1024]{2,1,0:T(8,128)(2,1)} %collective-permute-done.1, bf16[14,256,1024]{2,1,0:T(8,128)(2,1)} %bitcast.62, bf16[14,128,1024]{2,1,0:T(8,128)(2,1)} %collective-permute-done, f32[]{:T(128)S(6)} %sqrt.2, s32[64]{0:T(128)S(1)} %iota_multiply_fusion.2, s32[512]{0:T(512)S(1)} %iota_add_fusion), kind=kOutput, calls=%fused_computation | convolution fusion | flops 984154112 | bytes 18352388 | tf_op jit(solution)/shard_map/ir,brc->bic/dot_general | solution.py:76
  271.7 0.0 copy-done.7
  271.7 5.9 %fusion.15 = bf16[14,64,256]{2,1,0:T(8,128)(2,1)S(1)} fusion(f32[14,1024,64]{1,2,0:T(8,128)S(1)} %fusion, bf16[14,64,256]{2,1,0:T(8,128)(2,1)S(1)} %copy-done.7, f32[]{:T(128)S(6)} %sqrt.2, s32[256]{0:T(256)S(1)} %iota_multiply_fusion), kind=kOutput, calls=%fused_computation.20 | convolution fusion | flops 2823979008 | bytes 4588548 | tf_op jit(solution)/shard_map/bic,cj->bij/dot_general | solution.py:79
  277.7 0.0 copy-start.4
  277.7 23.1 %collective-permute-start.2 = (bf16[14,32,256]{2,1,0:T(8,128)(2,1)S(1)}, bf16[14,32,256]{2,1,0:T(8,128)(2,1)S(1)}, u32[]{:S(2)}, u32[]{:S(2)}) collective-permute-start(bf16[14,32,256]{2,1,0:T(8,128)(2,1)S(1)} %get-tuple-element.12), channel_id=1, source_target_pairs={{0,16},{16,32},{32,48},{48,64},{64,80},{80,96},{96,112},{112,128},... | collective-permute-start | bytes 688136 | tf_op jit(solution)/shard_map/ppermute | solution.py:19
  300.8 2.1 collective-permute-start.3
  303.0 5.4 %collective-permute-done.2 = bf16[14,32,256]{2,1,0:T(8,128)(2,1)S(1)} collective-permute-done((bf16[14,32,256]{2,1,0:T(8,128)(2,1)S(1)}, bf16[14,32,256]{2,1,0:T(8,128)(2,1)S(1)}, u32[]{:S(2)}, u32[]{:S(2)}) %collective-permute-start.2) | collective-permute-done | bytes 229408 | tf_op jit(solution)/shard_map/ppermute | solution.py:19
  308.4 4.7 collective-permute-done.3
  313.1 1.1 fusion.27
  314.3 16.4 %convolution_convert_fusion = bf16[14,256,1024]{2,1,0:T(8,128)(2,1)S(1)} fusion(f32[14,256,256]{2,1,0:T(8,128)S(1)} %fusion.27, f32[]{:T(128)S(6)} %sqrt.2, s32[256]{0:T(256)S(1)} %iota_multiply_fusion), kind=kOutput, calls=%fused_computation.9 | convolution fusion | flops 11282677760 | bytes 11011076 | tf_op jit(solution)/shard_map/brj,cj->brc/dot_general | solution.py:89
  330.7 0.0 copy-done.4
  330.7 7.5 %copy.34 = bf16[14,256,1024]{2,0,1:T(8,128)(2,1)} copy(bf16[14,256,1024]{2,1,0:T(8,128)(2,1)S(1)} %convolution_convert_fusion) | data formatting | bytes 14680064 | tf_op jit(solution)/shard_map/convert_element_type | solution.py:89
  338.2 0.0 copy-start.5
  338.2 0.0 copy-start.6
  338.2 5.3 %all-to-all-start.1 = ((bf16[14,256,1024]{2,0,1:T(8,128)(2,1)}), bf16[14,256,1024]{2,0,1:T(8,128)(2,1)}, u32[]{:S(2)}, u32[]{:S(2)}) async-start(bf16[14,256,1024]{2,0,1:T(8,128)(2,1)} %copy.34), calls=%async_computation.1 | async-start | bytes 16777216 | tf_op jit(solution)/shard_map/all_to_all | solution.py:92
  343.5 0.0 copy-done.5
  343.5 0.0 copy-done.6
  343.5 5.0 %fusion.19 = bf16[8,16,1024]{2,0,1:T(8,128)(2,1)S(1)} fusion(bf16[224,16,1024]{2,0,1:T(8,128)(2,1)} %copy-done.1, bf16[8,16,1024]{2,1,0:T(8,128)(2,1)S(1)} %copy-done.5, bf16[8,224]{1,0:T(8,128)(2,1)S(1)} %copy-done.6), kind=kOutput, calls=%fused_computation.23 | convolution fusion | flops 59113472 | bytes 7867904 | tf_op jit(solution)/shard_map/mb,brc->mrc/dot_general | solution.py:86
  348.5 89.9 %all-to-all-done.1 = bf16[14,256,1024]{2,0,1:T(8,128)(2,1)} async-done(((bf16[14,256,1024]{2,0,1:T(8,128)(2,1)}), bf16[14,256,1024]{2,0,1:T(8,128)(2,1)}, u32[]{:S(2)}, u32[]{:S(2)}) %all-to-all-start.1) | async-done | bytes 7340064 | tf_op jit(solution)/shard_map/all_to_all | solution.py:92
  438.4 7.5 %copy.35 = bf16[14,256,1024]{2,1,0:T(8,128)(2,1)S(1)} copy(bf16[14,256,1024]{2,0,1:T(8,128)(2,1)} %all-to-all-done.1) | data formatting | bytes 14680064 | tf_op jit(solution)/shard_map/all_to_all | solution.py:92
  445.9 7.1 %convert_bitcast_fusion = f32[16,14,16,1024]{3,2,0,1:T(8,128)} fusion(bf16[14,16,16,1024]{3,2,1,0:T(8,128)(2,1)S(1)} %bitcast.64), kind=kLoop, calls=%fused_computation.6 | loop fusion | flops 3670016 | bytes 22020096 | tf_op jit(solution)/shard_map/convert_element_type | solution.py:96
  453.0 0.0 copy-start.3
  453.0 13.7 %copy.36 = f32[16,14,16,1024]{3,2,1,0:T(8,128)} copy(f32[16,14,16,1024]{3,2,0,1:T(8,128)} %convert_bitcast_fusion) | data formatting | bytes 29360128 | tf_op jit(solution)/shard_map/convert_element_type | solution.py:96
  466.7 0.0 copy-done.3
  466.7 16.8 %fusion.11 = bf16[32,16,1024]{2,0,1:T(8,128)(2,1)S(1)} fusion(f32[224,16,1024]{2,1,0:T(8,128)} %bitcast.60, bf16[8,16,1024]{2,0,1:T(8,128)(2,1)S(1)} %fusion.19, bf16[32,16,1024]{2,1,0:T(8,128)(2,1)S(1)} %copy-done.3, bf16[224,32]{0,1:T(8,128)(2,1)S(1)} %copy-done, bf16[8,224]{1,0:T(8,128)(2,1)S(1)} %copy-done.6), kind=kOutput, calls=%fused_computation.16 | convolution fusion | flops 303038464 | bytes 17057280 | tf_op jit(solution)/shard_map/bk,brc->krc/dot_general | solution.py:97
  483.5 1.5 copy.39
  (5 shorter events, 0.0 us)
Async XLA Ops:
  0.6 0.7 copy-start
  4.7 7.1 %copy-start.1 = (bf16[224,16,1024]{2,0,1:T(8,128)(2,1)}, bf16[224,16,1024]{2,0,1:T(8,128)(2,1)S(1)}, u32[]{:S(2)}) copy-start(bf16[224,16,1024]{2,0,1:T(8,128)(2,1)S(1)} %convolution_convert_fusion.1) | copy-start | bytes 22020100
  106.3 5.7 %copy-start.2 = (bf16[14,16,16,1024]{3,2,1,0:T(8,128)(2,1)}, bf16[14,16,16,1024]{3,2,1,0:T(8,128)(2,1)S(1)}, u32[]{:S(2)}) copy-start(bf16[14,16,16,1024]{3,2,1,0:T(8,128)(2,1)S(1)} %copy.31) | copy-start | bytes 22020100
  112.0 87.0 %collective-permute-start = (bf16[14,128,1024]{2,1,0:T(8,128)(2,1)}, bf16[14,128,1024]{2,1,0:T(8,128)(2,1)}, u32[]{:S(2)}, u32[]{:S(2)}) collective-permute-start(bf16[14,128,1024]{2,1,0:T(8,128)(2,1)} %get-tuple-element.10), channel_id=1, source_target_pairs={{0,16},{16,32},{32,48},{48,64},{64,80},{80,96},{96,112},{112,128},... | collective-permute-start | bytes 11010056 | tf_op jit(solution)/shard_map/ppermute | solution.py:19
  117.2 146.4 %collective-permute-start.1 = (bf16[14,128,1024]{2,1,0:T(8,128)(2,1)}, bf16[14,128,1024]{2,1,0:T(8,128)(2,1)}, u32[]{:S(2)}, u32[]{:S(2)}) collective-permute-start(bf16[14,128,1024]{2,1,0:T(8,128)(2,1)} %get-tuple-element.11), channel_id=1, source_target_pairs={{16,0},{32,16},{48,32},{64,48},{80,64},{96,80},{112,96},{128,112},... | collective-permute-start | bytes 11010056 | tf_op jit(solution)/shard_map/ppermute | solution.py:21
  122.7 149.1 %copy-start.7 = (bf16[14,64,256]{2,1,0:T(8,128)(2,1)S(1)}, bf16[14,64,256]{2,1,0:T(8,128)(2,1)}, u32[]{:S(2)}) copy-start(bf16[14,64,256]{2,1,0:T(8,128)(2,1)} %param.8) | copy-start | bytes 1376260
  277.7 53.0 %copy-start.4 = (bf16[14,64,256]{2,1,0:T(8,128)(2,1)}, bf16[14,64,256]{2,1,0:T(8,128)(2,1)S(1)}, u32[]{:S(2)}) copy-start(bf16[14,64,256]{2,1,0:T(8,128)(2,1)S(1)} %fusion.15) | copy-start | bytes 1376260
  277.7 30.7 %collective-permute-start.2 = (bf16[14,32,256]{2,1,0:T(8,128)(2,1)S(1)}, bf16[14,32,256]{2,1,0:T(8,128)(2,1)S(1)}, u32[]{:S(2)}, u32[]{:S(2)}) collective-permute-start(bf16[14,32,256]{2,1,0:T(8,128)(2,1)S(1)} %get-tuple-element.12), channel_id=1, source_target_pairs={{0,16},{16,32},{32,48},{48,64},{64,80},{80,96},{96,112},{112,128},... | collective-permute-start | bytes 688136 | tf_op jit(solution)/shard_map/ppermute | solution.py:19
  300.8 12.3 %collective-permute-start.3 = (bf16[14,32,256]{2,1,0:T(8,128)(2,1)S(1)}, bf16[14,32,256]{2,1,0:T(8,128)(2,1)S(1)}, u32[]{:S(2)}, u32[]{:S(2)}) collective-permute-start(bf16[14,32,256]{2,1,0:T(8,128)(2,1)S(1)} %get-tuple-element.13), channel_id=1, source_target_pairs={{16,0},{32,16},{48,32},{64,48},{80,64},{96,80},{112,96},{128,112},... | collective-permute-start | bytes 688136 | tf_op jit(solution)/shard_map/ppermute | solution.py:21
  338.2 5.3 %copy-start.5 = (bf16[8,16,1024]{2,1,0:T(8,128)(2,1)S(1)}, bf16[8,16,1024]{2,1,0:T(8,128)(2,1)}, u32[]{:S(2)}) copy-start(bf16[8,16,1024]{2,1,0:T(8,128)(2,1)} %param.9) | copy-start | bytes 786436
  338.2 5.3 %copy-start.6 = (bf16[8,224]{1,0:T(8,128)(2,1)S(1)}, bf16[8,224]{1,0:T(8,128)(2,1)}, u32[]{:S(2)}) copy-start(bf16[8,224]{1,0:T(8,128)(2,1)} %param.7) | copy-start | bytes 10756
  338.2 100.2 %all-to-all-start.1 = ((bf16[14,256,1024]{2,0,1:T(8,128)(2,1)}), bf16[14,256,1024]{2,0,1:T(8,128)(2,1)}, u32[]{:S(2)}, u32[]{:S(2)}) async-start(bf16[14,256,1024]{2,0,1:T(8,128)(2,1)} %copy.34), calls=%async_computation.1 | async-start | bytes 16777216 | tf_op jit(solution)/shard_map/all_to_all | solution.py:92
  453.0 13.7 %copy-start.3 = (bf16[32,16,1024]{2,1,0:T(8,128)(2,1)S(1)}, bf16[32,16,1024]{2,1,0:T(8,128)(2,1)}, u32[]{:S(2)}) copy-start(bf16[32,16,1024]{2,1,0:T(8,128)(2,1)} %param.5) | copy-start | bytes 3145732
where the time goes:
time: 492 us; the launch traced here: 485 us
  waiting for transfers between devices  241 us (49%)
  blocking collectives  89.8 us (18%)
  matrix products  56.8 us (12%)
  local copies, waits for them, and re-layouts  48.5 us (10%)
  starting transfers between devices  39.8 us (8%)
  other arithmetic  7.76 us (2%)
    all_to_all x1, waiting for transfers between devices, shards(): lax.all_to_all(spread, 'spec', split_axis=1, concat_axis=0, tiled=True)  89.9 us
    all_to_all x1, blocking collectives, shards(): lax.all_to_all(spectra, 'spec', split_axis=0, concat_axis=1, tiled=True)  89.8 us
    ppermute x2, waiting for transfers between devices, with_halo(): lax.ppermute(tail, axis, [(i, (i + 1) % count) for i in range(ends)])  81.8 us
    ppermute x2, waiting for transfers between devices, with_halo(): lax.ppermute(head, axis, [((i + 1) % count, i) for i in range(ends)])  69.2 us
    ppermute x2, starting transfers between devices, with_halo(): lax.ppermute(tail, axis, [(i, (i + 1) % count) for i in range(ends)])  28.2 us
    dot_general x1, matrix products, shards(): jnp.einsum('bk,brc->krc', basis, spectral, preferred_element_type=jnp.flo...  16.8 us
    dot_general x1, matrix products, shards(): jnp.einsum('brj,cj->brc', rows_back, column_wide, precision=highest)  16.4 us
    convert_element_type x1, local copies, waits for them, and re-layouts, shards(): spread_pixel.astype(jnp.float32) + multi_back  13.7 us
  transfers between devices with their start and end apart: 5, of which 5 were waited for; matrix products, arithmetic and copies ran while one was open for 1% of the time, Pallas kernels for 0%

commit v1 on v0

--- a/solution.py
+++ b/solution.py
@@ -71,7 +71,10 @@
     )
     column_kernel = column_matrix(width_cols, width_cols // DECIM)
     column_wide = column_kernel.astype(jnp.float32)
-    band_cube = lax.all_to_all(spectra, "spec", split_axis=0, concat_axis=1, tiled=True)
+    band_cube = jnp.concatenate(
+        lax.all_to_all(jnp.stack(jnp.split(spectra, lax.axis_size("spec"), axis=0)), "spec", 0, 0),
+        axis=1,
+    )
     padded = with_halo(band_cube, (("tile", 1),), HALO)
     rows_done = jnp.einsum(
         "ir,brc->bic", row_matrix(rows_dev), padded, preferred_element_type=jnp.float32

time: 492 us -> 512 us (1.041)
  local copies, waits for them, and re-layouts: 48.5 us -> 67.5 us
  waiting for transfers between devices: 241 us -> 253 us
  starting transfers between devices: 39.8 us -> 27.8 us
    unnamed x17 -> x32, local copies, waits for them, and re-layouts: 3.15 us -> 20.5 us
    ppermute x2, starting transfers between devices: 28.2 us -> 16.5 us  [with_halo(): lax.ppermute(tail, axis, [(i, (i + 1) % count) for i in range(ends)])]
    ppermute x2, waiting for transfers between devices: 69.2 us -> 80.8 us  [with_halo(): lax.ppermute(head, axis, [((i + 1) % count, i) for i in range(ends)])]
    another operation x0 -> x2, local copies, waits for them, and re-layouts: none -> 9.23 us  [shards(): jnp.stack(jnp.split(spectra, lax.axis_size('spec'), axis=0))]
    convert_element_type x1 -> x0, local copies, waits for them, and re-layouts: 7.11 us -> none  [shards(): jnp.einsum('bk,krc->brc', basis, latent, preferred_element_type=jnp.float32)]
where the time goes in v1:
time: 512 us; the launch traced here: 504 us
  waiting for transfers between devices  253 us (49%)
  blocking collectives  89.7 us (18%)
  local copies, waits for them, and re-layouts  67.5 us (13%)
  matrix products  56.8 us (11%)
  starting transfers between devices  27.8 us (5%)
  other arithmetic  7.76 us (2%)
    all_to_all x1, waiting for transfers between devices, shards(): lax.all_to_all(spread, 'spec', split_axis=1, concat_axis=0, tiled=True)  89.9 us
    all_to_all x1, blocking collectives, shards(): lax.all_to_all(jnp.stack(jnp.split(spectra, lax.axis_size('spec'), axis=0...  89.7 us
    ppermute x2, waiting for transfers between devices, with_halo(): lax.ppermute(tail, axis, [(i, (i + 1) % count) for i in range(ends)])  81.9 us
    ppermute x2, waiting for transfers between devices, with_halo(): lax.ppermute(head, axis, [((i + 1) % count, i) for i in range(ends)])  80.8 us
    unnamed x32, local copies, waits for them, and re-layouts  20.5 us
    dot_general x1, matrix products, shards(): jnp.einsum('bk,brc->krc', basis, spectral, preferred_element_type=jnp.flo...  16.8 us
    ppermute x2, starting transfers between devices, with_halo(): lax.ppermute(tail, axis, [(i, (i + 1) % count) for i in range(ends)])  16.5 us
    dot_general x1, matrix products, shards(): jnp.einsum('brj,cj->brc', rows_back, column_wide, precision=highest)  16.4 us
  transfers between devices with their start and end apart: 5, of which 5 were waited for; matrix products, arithmetic and copies ran while one was open for 1% of the time, Pallas kernels for 0%

profile of v1, /device:TPU:16, one launch (start us, length us, event | category | flops | bytes accessed | tf_op | source)
XLA Modules:
  0.0 504.0 jit_solution(15301786171406721684)
XLA Ops:
  0.6 0.0 copy-start
  0.6 0.7 copy-done
  1.4 3.3 convolution_convert_fusion.1
  4.7 0.9 fusion.49
  5.6 1.5 fusion.48
  7.1 1.1 fusion.47
  8.2 1.1 fusion.46
  9.2 0.8 fusion.45
  10.1 1.0 fusion.44
  11.1 1.0 fusion.43
  12.1 1.0 fusion.42
  13.1 0.8 fusion.41
  14.0 1.0 fusion.40
  15.0 1.0 fusion.39
  16.0 1.0 fusion.38
  17.1 0.9 fusion.37
  17.9 1.0 fusion.36
  18.9 1.0 fusion.35
  19.9 1.0 fusion.34
  20.9 8.3 %copy.28 = bf16[16,14,16,1024]{3,2,1,0:T(8,128)(2,1)S(1)} copy(bf16[16,14,16,1024]{3,1,2,0:T(8,128)(2,1)} %fusion.34) | data formatting | bytes 14680064 | tf_op jit(solution)/shard_map/stack | solution.py:75
  29.2 89.7 %all_to_all.14 = bf16[16,14,16,1024]{3,2,1,0:T(8,128)(2,1)} all-to-all(bf16[16,14,16,1024]{3,2,1,0:T(8,128)(2,1)S(1)} %copy.28), channel_id=1, replica_groups=mesh['tile'=16,'spec'=16] {'spec'}, dimensions={0} | all-to-all | bytes 14680064 | tf_op jit(solution)/shard_map/all_to_all | solution.py:75
  118.9 4.7 copy.29
  123.6 3.0 copy-done.2
  126.6 4.3 fusion.135
  131.0 5.2 %collective-permute-start = (bf16[14,128,1024]{2,1,0:T(8,128)(2,1)}, bf16[14,128,1024]{2,1,0:T(8,128)(2,1)}, u32[]{:S(2)}, u32[]{:S(2)}) collective-permute-start(bf16[14,128,1024]{2,1,0:T(8,128)(2,1)} %get-tuple-element.10), channel_id=1, source_target_pairs={{0,16},{16,32},{32,48},{48,64},{64,80},{80,96},{96,112},{112,128},... | collective-permute-start | bytes 11010056 | tf_op jit(solution)/shard_map/ppermute | solution.py:19
  136.1 3.9 collective-permute-start.1
  140.1 0.7 fusion.108
  141.5 0.0 copy-start.7
  141.5 76.5 %collective-permute-done = bf16[14,128,1024]{2,1,0:T(8,128)(2,1)} collective-permute-done((bf16[14,128,1024]{2,1,0:T(8,128)(2,1)}, bf16[14,128,1024]{2,1,0:T(8,128)(2,1)}, u32[]{:S(2)}, u32[]{:S(2)}) %collective-permute-start) | collective-permute-done | bytes 3670048 | tf_op jit(solution)/shard_map/ppermute | solution.py:19
  218.0 76.1 %collective-permute-done.1 = bf16[14,128,1024]{2,1,0:T(8,128)(2,1)} collective-permute-done((bf16[14,128,1024]{2,1,0:T(8,128)(2,1)}, bf16[14,128,1024]{2,1,0:T(8,128)(2,1)}, u32[]{:S(2)}, u32[]{:S(2)}) %collective-permute-start.1) | collective-permute-done | bytes 3670048 | tf_op jit(solution)/shard_map/ppermute | solution.py:21
  294.1 8.2 %fusion = f32[14,1024,64]{1,2,0:T(8,128)S(1)} fusion(bf16[14,128,1024]{2,1,0:T(8,128)(2,1)} %collective-permute-done.1, bf16[14,256,1024]{2,1,0:T(8,128)(2,1)} %bitcast.124, bf16[14,128,1024]{2,1,0:T(8,128)(2,1)} %collective-permute-done, f32[]{:T(128)S(6)} %sqrt.2, s32[64]{0:T(128)S(1)} %iota_multiply_fusion.2, s32[512]{0:T(512)S(1)} %iota_add_fusion), kind=kOutput, calls=%fused_computation | convolution fusion | flops 984154112 | bytes 18352388 | tf_op jit(solution)/shard_map/ir,brc->bic/dot_general | solution.py:79
  302.3 5.9 %fusion.15 = bf16[14,64,256]{2,1,0:T(8,128)(2,1)S(1)} fusion(f32[14,1024,64]{1,2,0:T(8,128)S(1)} %fusion, bf16[14,64,256]{2,1,0:T(8,128)(2,1)S(1)} %copy-done.7, f32[]{:T(128)S(6)} %sqrt.2, s32[256]{0:T(256)S(1)} %iota_multiply_fusion), kind=kOutput, calls=%fused_computation.20 | convolution fusion | flops 2823979008 | bytes 4588548 | tf_op jit(solution)/shard_map/bic,cj->bij/dot_general | solution.py:82
  308.2 0.0 copy-start.4
  308.3 11.3 %collective-permute-start.2 = (bf16[14,32,256]{2,1,0:T(8,128)(2,1)S(1)}, bf16[14,32,256]{2,1,0:T(8,128)(2,1)S(1)}, u32[]{:S(2)}, u32[]{:S(2)}) collective-permute-start(bf16[14,32,256]{2,1,0:T(8,128)(2,1)S(1)} %get-tuple-element.12), channel_id=1, source_target_pairs={{0,16},{16,32},{32,48},{48,64},{64,80},{80,96},{96,112},{112,128},... | collective-permute-start | bytes 688136 | tf_op jit(solution)/shard_map/ppermute | solution.py:19
  319.6 2.1 collective-permute-start.3
  321.8 5.4 %collective-permute-done.2 = bf16[14,32,256]{2,1,0:T(8,128)(2,1)S(1)} collective-permute-done((bf16[14,32,256]{2,1,0:T(8,128)(2,1)S(1)}, bf16[14,32,256]{2,1,0:T(8,128)(2,1)S(1)}, u32[]{:S(2)}, u32[]{:S(2)}) %collective-permute-start.2) | collective-permute-done | bytes 229408 | tf_op jit(solution)/shard_map/ppermute | solution.py:19
  327.2 4.7 collective-permute-done.3
  331.9 1.1 fusion.27
  333.0 16.4 %convolution_convert_fusion = bf16[14,256,1024]{2,1,0:T(8,128)(2,1)S(1)} fusion(f32[14,256,256]{2,1,0:T(8,128)S(1)} %fusion.27, f32[]{:T(128)S(6)} %sqrt.2, s32[256]{0:T(256)S(1)} %iota_multiply_fusion), kind=kOutput, calls=%fused_computation.9 | convolution fusion | flops 11282677760 | bytes 11011076 | tf_op jit(solution)/shard_map/brj,cj->brc/dot_general | solution.py:92
  349.5 7.5 %copy.32 = bf16[14,256,1024]{2,0,1:T(8,128)(2,1)} copy(bf16[14,256,1024]{2,1,0:T(8,128)(2,1)S(1)} %convolution_convert_fusion) | data formatting | bytes 14680064 | tf_op jit(solution)/shard_map/convert_element_type | solution.py:92
  357.0 5.3 %all-to-all-start.1 = ((bf16[14,256,1024]{2,0,1:T(8,128)(2,1)}), bf16[14,256,1024]{2,0,1:T(8,128)(2,1)}, u32[]{:S(2)}, u32[]{:S(2)}) async-start(bf16[14,256,1024]{2,0,1:T(8,128)(2,1)} %copy.32), calls=%async_computation.1 | async-start | bytes 16777216 | tf_op jit(solution)/shard_map/all_to_all | solution.py:95
  362.3 5.0 fusion.19
  367.2 89.9 %all-to-all-done.1 = bf16[14,256,1024]{2,0,1:T(8,128)(2,1)} async-done(((bf16[14,256,1024]{2,0,1:T(8,128)(2,1)}), bf16[14,256,1024]{2,0,1:T(8,128)(2,1)}, u32[]{:S(2)}, u32[]{:S(2)}) %all-to-all-start.1) | async-done | bytes 7340064 | tf_op jit(solution)/shard_map/all_to_all | solution.py:95
  457.1 7.5 %copy.33 = bf16[14,256,1024]{2,1,0:T(8,128)(2,1)S(1)} copy(bf16[14,256,1024]{2,0,1:T(8,128)(2,1)} %all-to-all-done.1) | data formatting | bytes 14680064 | tf_op jit(solution)/shard_map/all_to_all | solution.py:95
  464.6 7.1 %convert_bitcast_fusion = f32[16,14,16,1024]{3,2,0,1:T(8,128)} fusion(bf16[14,16,16,1024]{3,2,1,0:T(8,128)(2,1)S(1)} %bitcast.126), kind=kLoop, calls=%fused_computation.6 | loop fusion | flops 3670016 | bytes 22020096 | tf_op jit(solution)/shard_map/convert_element_type | solution.py:99
  471.7 13.7 %copy.34 = f32[16,14,16,1024]{3,2,1,0:T(8,128)} copy(f32[16,14,16,1024]{3,2,0,1:T(8,128)} %convert_bitcast_fusion) | data formatting | bytes 29360128 | tf_op jit(solution)/shard_map/convert_element_type | solution.py:99
  485.4 16.8 %fusion.11 = bf16[32,16,1024]{2,0,1:T(8,128)(2,1)S(1)} fusion(f32[224,16,1024]{2,1,0:T(8,128)} %bitcast.122, bf16[8,16,1024]{2,0,1:T(8,128)(2,1)S(1)} %fusion.19, bf16[32,16,1024]{2,1,0:T(8,128)(2,1)S(1)} %copy-done.3, bf16[224,32]{0,1:T(8,128)(2,1)S(1)} %copy-done, bf16[8,224]{1,0:T(8,128)(2,1)S(1)} %copy-done.6), kind=kOutput, calls=%fused_computation.16 | convolution fusion | flops 303038464 | bytes 17057280 | tf_op jit(solution)/shard_map/bk,brc->krc/dot_general | solution.py:100
  502.2 1.5 copy.37
  (16 shorter events, 0.1 us)
Async XLA Ops:
  0.6 0.7 copy-start
  4.7 15.2 %copy-start.1 = (bf16[224,16,1024]{2,0,1:T(8,128)(2,1)}, bf16[224,16,1024]{2,0,1:T(8,128)(2,1)S(1)}, u32[]{:S(2)}) copy-start(bf16[224,16,1024]{2,0,1:T(8,128)(2,1)S(1)} %convolution_convert_fusion.1) | copy-start | bytes 22020100
  123.6 3.0 copy-start.2
  131.0 87.0 %collective-permute-start = (bf16[14,128,1024]{2,1,0:T(8,128)(2,1)}, bf16[14,128,1024]{2,1,0:T(8,128)(2,1)}, u32[]{:S(2)}, u32[]{:S(2)}) collective-permute-start(bf16[14,128,1024]{2,1,0:T(8,128)(2,1)} %get-tuple-element.10), channel_id=1, source_target_pairs={{0,16},{16,32},{32,48},{48,64},{64,80},{80,96},{96,112},{112,128},... | collective-permute-start | bytes 11010056 | tf_op jit(solution)/shard_map/ppermute | solution.py:19
  136.1 158.0 %collective-permute-start.1 = (bf16[14,128,1024]{2,1,0:T(8,128)(2,1)}, bf16[14,128,1024]{2,1,0:T(8,128)(2,1)}, u32[]{:S(2)}, u32[]{:S(2)}) collective-permute-start(bf16[14,128,1024]{2,1,0:T(8,128)(2,1)} %get-tuple-element.11), channel_id=1, source_target_pairs={{16,0},{32,16},{48,32},{64,48},{80,64},{96,80},{112,96},{128,112},... | collective-permute-start | bytes 11010056 | tf_op jit(solution)/shard_map/ppermute | solution.py:21
  141.5 160.8 %copy-start.7 = (bf16[14,64,256]{2,1,0:T(8,128)(2,1)S(1)}, bf16[14,64,256]{2,1,0:T(8,128)(2,1)}, u32[]{:S(2)}) copy-start(bf16[14,64,256]{2,1,0:T(8,128)(2,1)} %param.8) | copy-start | bytes 1376260
  308.2 41.2 %copy-start.4 = (bf16[14,64,256]{2,1,0:T(8,128)(2,1)}, bf16[14,64,256]{2,1,0:T(8,128)(2,1)S(1)}, u32[]{:S(2)}) copy-start(bf16[14,64,256]{2,1,0:T(8,128)(2,1)S(1)} %fusion.15) | copy-start | bytes 1376260
  308.3 18.9 %collective-permute-start.2 = (bf16[14,32,256]{2,1,0:T(8,128)(2,1)S(1)}, bf16[14,32,256]{2,1,0:T(8,128)(2,1)S(1)}, u32[]{:S(2)}, u32[]{:S(2)}) collective-permute-start(bf16[14,32,256]{2,1,0:T(8,128)(2,1)S(1)} %get-tuple-element.12), channel_id=1, source_target_pairs={{0,16},{16,32},{32,48},{48,64},{64,80},{80,96},{96,112},{112,128},... | collective-permute-start | bytes 688136 | tf_op jit(solution)/shard_map/ppermute | solution.py:19
  319.6 12.3 %collective-permute-start.3 = (bf16[14,32,256]{2,1,0:T(8,128)(2,1)S(1)}, bf16[14,32,256]{2,1,0:T(8,128)(2,1)S(1)}, u32[]{:S(2)}, u32[]{:S(2)}) collective-permute-start(bf16[14,32,256]{2,1,0:T(8,128)(2,1)S(1)} %get-tuple-element.13), channel_id=1, source_target_pairs={{16,0},{32,16},{48,32},{64,48},{80,64},{96,80},{112,96},{128,112},... | collective-permute-start | bytes 688136 | tf_op jit(solution)/shard_map/ppermute | solution.py:21
  357.0 5.3 %copy-start.5 = (bf16[8,16,1024]{2,1,0:T(8,128)(2,1)S(1)}, bf16[8,16,1024]{2,1,0:T(8,128)(2,1)}, u32[]{:S(2)}) copy-start(bf16[8,16,1024]{2,1,0:T(8,128)(2,1)} %param.9) | copy-start | bytes 786436
  357.0 5.3 %copy-start.6 = (bf16[8,224]{1,0:T(8,128)(2,1)S(1)}, bf16[8,224]{1,0:T(8,128)(2,1)}, u32[]{:S(2)}) copy-start(bf16[8,224]{1,0:T(8,128)(2,1)} %param.7) | copy-start | bytes 10756
  357.0 100.2 %all-to-all-start.1 = ((bf16[14,256,1024]{2,0,1:T(8,128)(2,1)}), bf16[14,256,1024]{2,0,1:T(8,128)(2,1)}, u32[]{:S(2)}, u32[]{:S(2)}) async-start(bf16[14,256,1024]{2,0,1:T(8,128)(2,1)} %copy.32), calls=%async_computation.1 | async-start | bytes 16777216 | tf_op jit(solution)/shard_map/all_to_all | solution.py:95
  471.7 13.7 %copy-start.3 = (bf16[32,16,1024]{2,1,0:T(8,128)(2,1)S(1)}, bf16[32,16,1024]{2,1,0:T(8,128)(2,1)}, u32[]{:S(2)}) copy-start(bf16[32,16,1024]{2,1,0:T(8,128)(2,1)} %param.5) | copy-start | bytes 3145732
